TPU v7x, 32 devices: a whole 2x2x4 slice. The times are simulated.
32 devices in a mesh: groups: 2 (over y), events: 8 (over z, x), heads: 2 (over core).
Axes of the slice: x: 2, y: 2, z: 4, core: 2. Of those that a mesh axis runs over, the one named last changes fastest.
Arguments:
- inputs: bfloat16 [256, 1024], P(('groups', 'events')), parts along dimension 0, may hold values from -6 to 6
- cand_user: int32 [256], P('groups'), parts along dimension 0, may hold values from 0 to 3, as said below
- event_user: int32 [8192], P(('groups', 'events')), parts along dimension 0, may hold values from 0 to 3, as said below
- event_count: int32 [16], P(('groups', 'events')), parts along dimension 0, may hold values from 128 to 512, as said below
- w_qu: bfloat16 [1024, 2, 1024], P(None, None, 'heads'), may hold values from -0.1875 to 0.1875
- keys: bfloat16 [8192, 1024], P(('groups', 'events'), 'heads'), parts along dimension 0, may hold values from -6 to 6
- values: bfloat16 [8192, 1024], P(('groups', 'events'), 'heads'), parts along dimension 0, may hold values from -6 to 6
- gain: float32 [1024], P('heads'), may hold values from 0.1 to 1.9
- w_out: bfloat16 [1024, 1024], P('heads'), may hold values from -0.1875 to 0.1875
Outputs:
- scored: bfloat16 [256, 1024], P(('groups', 'events')), parts along dimension 0
There are 2 independent parts, one for each index of `groups`. A program takes and returns all parts, laid end to end along the dimension named above; an argument that names none is the same for every part. Nothing has to cross between parts.
Inputs may be any that keep to these rules, and one draw needn't show every extreme that they name: `event_count`: each cache shard's filled slots come first; some shard is full and some holds 128. `event_user`: Users' events are consecutive and in increasing user order over the whole cache; every user has 1 to 2047 events, and some user has exactly 2047. `cand_user`: every candidate belongs to a user that has at least one filled slot somewhere in the cache.
All inputs are finite; a program needn't handle non-finite values.
Results may differ from a plain program's by a relative error of at most 0.0075.
Values may be sent and summed in bfloat16 or wider, within the bound.
No kernel may reach another device: no remote copies, remote signals or barrier semaphores. Data moves between devices by JAX's collectives and lax.ppermute only.
A program may use at most 64 MiB of HBM per device.

v0:
```python
import math
import jax
import jax.numpy as jnp
from jax import lax
from jax.sharding import PartitionSpec as P

DH = 128
HD = 1024
epsilon = 1e-05


def shards(inputs, cand_user, event_user, event_count, w_qu, keys, values, gain, w_out):
    row_count = inputs.shape[0]
    feat_width = inputs.shape[1]
    local_width = w_qu.shape[2]
    heads_here = local_width // DH
    slot_total = keys.shape[0]
    score_scale = 1.0 / math.sqrt(DH)
    packed_weight = w_qu.reshape(feat_width, 2 * local_width)
    query_weight = packed_weight[:, :local_width]
    gate_weight = packed_weight[:, local_width:]
    gate_values = jax.nn.silu(
        jnp.dot(inputs, gate_weight, preferred_element_type=jnp.float32)
    ).astype(jnp.bfloat16)
    gathered_rows = lax.all_gather(inputs, "events", axis=0, tiled=True)
    queries = jax.nn.silu(
        jnp.dot(gathered_rows, query_weight, preferred_element_type=jnp.float32)
    ).astype(jnp.bfloat16)
    slot_index = jnp.arange(slot_total, dtype=jnp.int32)
    slot_valid = slot_index < event_count[0]
    key_heads = keys.reshape(slot_total, heads_here, DH)
    value_heads = values.reshape(slot_total, heads_here, DH)

    def attend_rows(query_rows, row_users):
        rows_here = query_rows.shape[0]
        query_block = query_rows.reshape(rows_here, heads_here, DH)
        user_match = ((row_users[:, None] == event_user[None, :]) & slot_valid[None, :]).astype(
            jnp.float32
        )
        scores = (
            jnp.einsum("chd,ehd->hce", query_block, key_heads, preferred_element_type=jnp.float32)
            * score_scale
        )
        attn_weights = (jax.nn.silu(scores) * user_match[None]).astype(jnp.bfloat16)
        partial_out = jnp.einsum(
            "hce,ehd->chd", attn_weights, value_heads, preferred_element_type=jnp.float32
        )
        return partial_out.reshape(rows_here, local_width)

    block_rows = math.gcd(row_count * lax.axis_size("events"), 512)
    block_count = row_count * lax.axis_size("events") // block_rows

    def compute_block(which_block):
        block_start = which_block * block_rows
        query_rows = lax.dynamic_slice_in_dim(queries, block_start, block_rows, 0)
        block_users = lax.dynamic_slice_in_dim(cand_user, block_start, block_rows, 0)
        return attend_rows(query_rows, block_users)

    stacked = lax.map(compute_block, jnp.arange(block_count, dtype=jnp.int32))
    attended = lax.psum_scatter(
        stacked.reshape(row_count * lax.axis_size("events"), local_width),
        "events",
        scatter_dimension=0,
        tiled=True,
    )
    first_moment = jnp.sum(attended, axis=1)
    second_moment = jnp.sum(attended * attended, axis=1)
    total_first, total_second = lax.psum((first_moment, second_moment), "heads")
    average = total_first / HD
    variance = total_second / HD - average * average
    normed = (attended - average[:, None]) * lax.rsqrt(variance + epsilon)[:, None] * gain
    gated = (normed * gate_values.astype(jnp.float32)).astype(jnp.bfloat16)
    projected = jnp.dot(gated, w_out, preferred_element_type=jnp.float32)
    summed_heads = lax.psum(projected, "heads")
    return (inputs.astype(jnp.float32) + summed_heads).astype(jnp.bfloat16)


def solution(mesh):
    placed = (
        P(("groups", "events"), None),
        P("groups"),
        P(("groups", "events")),
        P(("groups", "events")),
        P(None, None, "heads"),
        P(("groups", "events"), "heads"),
        P(("groups", "events"), "heads"),
        P("heads"),
        P("heads", None),
    )
    return jax.shard_map(
        shards, mesh=mesh, in_specs=placed, out_specs=P(("groups", "events"), None), check_vma=False
    )
```

profile of v0, /device:TPU:0, one launch (start us, length us, event | category | flops | bytes accessed | tf_op | source)
XLA Modules:
  0.0 143.9 jit_solution(11439747766623471906)
XLA Ops:
  6.5 0.0 copy-start
  6.5 0.0 reduce-scatter.2.cloned.1.call-start
  7.3 32.8 %all_gather.3 = bf16[128,1024]{1,0:T(8,128)(2,1)S(1)} all-gather(bf16[16,1024]{1,0:T(8,128)(2,1)} %param.9), channel_id=1, replica_groups=mesh['groups'=2,'events'=8,'heads'=2] {'events'}, dimensions={0}, use_global_device_ids=true | all-gather | bytes 294912 | tf_op jit(solution)/shard_map/all_gather | solution.py:25
  40.1 2.0 %copy.14 = bf16[512,512]{0,1:T(8,128)(2,1)} copy(bf16[512,512]{1,0:T(8,128)(2,1)} %param.15) | data formatting | bytes 1048576 | tf_op jit(solution)/shard_map/reshape | solution.py:32
  42.1 2.2 %copy.17 = bf16[128,8,2,512]{3,1,2,0:T(8,128)(2,1)S(1)} copy(bf16[128,8,2,512]{3,2,1,0:T(2,128)(2,1)} %bitcast.29) | data formatting | bytes 4194304
  44.3 0.0 copy-start.2
  44.3 0.0 copy-start.4
  44.3 1.0 fusion.14
  45.3 0.0 copy-done.2
  45.3 0.0 copy-done.4
  45.3 0.1 and_convert_fusion
  45.4 0.0 copy-start.1
  45.4 0.0 copy-start.3
  45.4 2.6 %fusion.4 = f32[4,128,128]{1,2,0:T(8,128)} fusion(bf16[512,4,128]{0,2,1:T(8,128)(2,1)} %bitcast.30, f32[128,512]{1,0:T(8,128)S(1)} %and_convert_fusion, bf16[16,4,8,128]{3,2,1,0:T(8,128)(2,1)} %fusion.14, bf16[512,512]{1,0:T(8,128)(2,1)} %param.14), kind=kOutput, calls=%fused_computation.6 | convolution fusion | flops 136052736 | bytes 1703936 | tf_op jit(solution)/shard_map/while/body/eval_jaxpr/hce,ehd->chd/dot_general | solution.py:45
  48.1 1.8 %copy.13 = f32[128,512]{1,0:T(8,128)} copy(f32[128,512]{0,1:T(8,128)} %bitcast.31) | data formatting | bytes 524288 | tf_op jit(solution)/shard_map/reshape | solution.py:61
  49.9 0.0 reduce-scatter.2.cloned.1.call-update
  49.9 0.0 all-reduce.3.cloned.1.call-start
  49.9 63.5 %reduce-scatter.2.cloned.1.call-done = f32[16,512]{1,0:T(8,128)} async-done(((f32[128,512]{1,0:T(8,128)}), f32[16,512]{1,0:T(8,128)}) %reduce-scatter.2.cloned.1.call-update) | async-done | bytes 32784 | tf_op jit(solution)/shard_map/reduce_scatter | solution.py:60
  113.5 0.9 fusion.38
  114.3 2.5 %all-reduce = (f32[16]{0:T(128)S(1)}, f32[16]{0:T(128)S(1)}) all-reduce(f32[16]{0:T(128)S(1)} %get-tuple-element.20, f32[16]{0:T(128)S(1)} %get-tuple-element.19), channel_id=1, replica_groups=mesh['groups'=2,'events'=8,'heads'=2] {'heads'}, use_global_device_ids=true, to_apply=%region_4.5 | all-reduce | flops 32 | bytes 256 | tf_op jit(solution)/shard_map/psum | solution.py:68
  116.8 0.0 copy-done
  116.8 0.0 copy-done.1
  116.8 0.0 copy-done.3
  116.8 1.9 %fusion.26 = f32[16,1024]{1,0:T(8,128)} fusion(bf16[512,1024]{1,0:T(8,128)(2,1)S(1)} %copy-done, bf16[16,1024]{1,0:T(8,128)(2,1)S(1)} %copy-done.1, bf16[1024,1024]{1,0:T(8,128)(2,1)S(1)} %bitcast.28, f32[16,512]{1,0:T(8,128)} %reduce-scatter.2.cloned.1.call-done, f32[512]{0:T(512)S(1)} %copy-done.3, f32[16]{0:T(128)S(1)} %get-tuple-element.32, ...), kind=kOutput, calls=%fused_computation.20 | convolution fusion | flops 33644544 | bytes 2231296 | tf_op jit(solution)/shard_map/dot_general | solution.py:73
  118.7 0.0 all-reduce.3.cloned.1.call-update
  118.7 16.9 %all-reduce.3.cloned.1.call-done = f32[16,1024]{1,0:T(8,128)} async-done(((f32[16,1024]{1,0:T(8,128)}), f32[16,1024]{1,0:T(8,128)}) %all-reduce.3.cloned.1.call-update) | async-done | bytes 65552 | tf_op jit(solution)/shard_map/psum | solution.py:74
  135.6 1.5 %add_convert_fusion = bf16[16,1024]{1,0:T(8,128)(2,1)} fusion(f32[16,1024]{1,0:T(8,128)} %all-reduce.3.cloned.1.call-done, bf16[16,1024]{1,0:T(8,128)(2,1)S(1)} %copy-done.1), kind=kLoop, calls=%fused_computation.17 | loop fusion | flops 49152 | bytes 131072 | tf_op jit(solution)/shard_map/convert_element_type | solution.py:75
  (2 shorter events, 0.0 us)
Async XLA Ops:
  6.5 110.3 %copy-start = (bf16[512,1024]{1,0:T(8,128)(2,1)S(1)}, bf16[512,1024]{1,0:T(8,128)(2,1)}, u32[]{:S(2)}) copy-start(bf16[512,1024]{1,0:T(8,128)(2,1)} %param.17) | copy-start | bytes 3145732
  6.5 106.9 %reduce-scatter.2.cloned.1.call-start = ((), (), s32[]{:S(2)}) async-start(), calls=%async_computation.1 | async-start | bytes 294912 | tf_op jit(solution)/shard_map/reduce_scatter | solution.py:60
  44.3 1.0 copy-start.2
  44.3 1.0 copy-start.4
  45.4 71.4 %copy-start.1 = (bf16[16,1024]{1,0:T(8,128)(2,1)S(1)}, bf16[16,1024]{1,0:T(8,128)(2,1)}, u32[]{:S(2)}) copy-start(bf16[16,1024]{1,0:T(8,128)(2,1)} %param.9) | copy-start | bytes 98308
  45.4 71.4 %copy-start.3 = (f32[512]{0:T(512)S(1)}, f32[512]{0:T(512)}, u32[]{:S(2)}) copy-start(f32[512]{0:T(512)} %param.16) | copy-start | bytes 6148
  49.9 85.7 %all-reduce.3.cloned.1.call-start = ((), (), s32[]{:S(2)}) async-start(), calls=%async_computation.2 | async-start | bytes 131072 | tf_op jit(solution)/shard_map/psum | solution.py:74
Sparse Core Ops, SparseCore 0:
  50.0 63.4 reduce-scatter.1
  118.8 16.7 all-reduce.2
where the time goes:
time: 144 us
  waiting for transfers between devices  80.5 us (56%)
  blocking collectives  35.2 us (24%)
  between operations  14.2 us (10%)
  local copies, waits for them, and re-layouts  6 us (4%)
  matrix products  5.52 us (4%)
  other arithmetic  2.45 us (2%)
    reduce_scatter x1, waiting for transfers between devices, shards(): lax.psum_scatter(stacked.reshape(row_count * lax.axis_size('events'), loc...  63.5 us
    all_gather x1, blocking collectives, shards(): gathered_rows = lax.all_gather(inputs, 'events', axis=0, tiled=True)  32.8 us
    psum x1, waiting for transfers between devices, shards(): summed_heads = lax.psum(projected, 'heads')  16.9 us
  transfers between devices with their start and end apart: 2, of which 2 were waited for; matrix products, arithmetic and copies ran while one was open for 0% of the time, Pallas kernels for 0%

commit v1 on v0

--- a/solution.py
+++ b/solution.py
@@ -7,6 +7,27 @@
 DH = 128
 HD = 1024
 epsilon = 1e-05
+
+
+def collect(value, axis, dim):
+    size, position, rows = (lax.axis_size(axis), lax.axis_index(axis), value.shape[dim])
+    right = [(i, (i + 1) % size) for i in range(size)]
+    behind = [(i, (i - 1) % size) for i in range(size)]
+    filled = jnp.zeros((*value.shape[:dim], size * rows, *value.shape[dim + 1 :]), value.dtype)
+    filled = lax.dynamic_update_slice_in_dim(filled, value, position * rows, axis=dim)
+    from_left = from_right = value
+    halfway = size // 2
+    for hop in range(1, halfway + 1):
+        from_left = lax.ppermute(from_left, axis, right)
+        filled = lax.dynamic_update_slice_in_dim(
+            filled, from_left, (position - hop) % size * rows, axis=dim
+        )
+        if hop < size - halfway:
+            from_right = lax.ppermute(from_right, axis, behind)
+            filled = lax.dynamic_update_slice_in_dim(
+                filled, from_right, (position + hop) % size * rows, axis=dim
+            )
+    return filled
 
 
 def shards(inputs, cand_user, event_user, event_count, w_qu, keys, values, gain, w_out):
@@ -22,7 +43,7 @@
     gate_values = jax.nn.silu(
         jnp.dot(inputs, gate_weight, preferred_element_type=jnp.float32)
     ).astype(jnp.bfloat16)
-    gathered_rows = lax.all_gather(inputs, "events", axis=0, tiled=True)
+    gathered_rows = collect(inputs, "events", 0)
     queries = jax.nn.silu(
         jnp.dot(gathered_rows, query_weight, preferred_element_type=jnp.float32)
     ).astype(jnp.bfloat16)

time: 144 us -> 138 us (0.958)
  blocking collectives: 35.2 us -> 2.46 us
  starting transfers between devices: 0.04 us -> 15.5 us
  local copies, waits for them, and re-layouts: 6 us -> 12.4 us
  waiting for transfers between devices: 80.5 us -> 83.3 us
    all_gather x1 -> x0, blocking collectives: 32.8 us -> none  [shards(): gathered_rows = lax.all_gather(inputs, 'events', axis=0, tiled=True)]
    ppermute x0 -> x7, starting transfers between devices: none -> 15.5 us  [the longest x3 12.5 us: collect(): from_right = lax.ppermute(from_right, axis, behind)]
    ppermute x0 -> x7, waiting for transfers between devices: none -> 6.72 us  [the longest x4 6.71 us: collect(): from_left = lax.ppermute(from_left, axis, right)]
    dynamic_update_slice x0 -> x8, local copies, waits for them, and re-layouts: none -> 5.65 us  [the longest x4 2.45 us: collect(): lax.dynamic_update_slice_in_dim(filled, from_left, (position - hop) % siz...]
    reduce_scatter x1, waiting for transfers between devices: 63.5 us -> 59.6 us  [shards(): lax.psum_scatter(stacked.reshape(row_count * lax.axis_size('events'), loc...]
  transfers between devices with their start and end apart: 2 -> 9, of which waited for: 2 -> 5; matrix products, arithmetic and copies ran while one was open for 0% -> 8% of each run, Pallas kernels for 0% -> 0%
where the time goes in v1:
time: 138 us; the launch traced here: 137 us
  waiting for transfers between devices  83.3 us (60%)
  starting transfers between devices  15.5 us (11%)
  between operations  14.2 us (10%)
  local copies, waits for them, and re-layouts  12.4 us (9%)
  matrix products  6.46 us (5%)
  other arithmetic  3.14 us (2%)
  blocking collectives  2.46 us (2%)
    reduce_scatter x1, waiting for transfers between devices, shards(): lax.psum_scatter(stacked.reshape(row_count * lax.axis_size('events'), loc...  59.6 us
    psum x1, waiting for transfers between devices, shards(): summed_heads = lax.psum(projected, 'heads')  16.9 us
    ppermute x3, starting transfers between devices, collect(): from_right = lax.ppermute(from_right, axis, behind)  12.5 us
    ppermute x4, waiting for transfers between devices, collect(): from_left = lax.ppermute(from_left, axis, right)  6.71 us
    ppermute x4, starting transfers between devices, collect(): from_left = lax.ppermute(from_left, axis, right)  3.03 us
  transfers between devices with their start and end apart: 9, of which 5 were waited for; matrix products, arithmetic and copies ran while one was open for 8% of the time, Pallas kernels for 0%

profile of v1, /device:TPU:0, one launch (start us, length us, event | category | flops | bytes accessed | tf_op | source)
XLA Modules:
  0.0 137.4 jit_solution(7435239161077311004)
XLA Ops:
  6.5 0.0 copy-start
  6.5 0.0 reduce-scatter.2.cloned.1.call-start
  6.5 3.0 %collective-permute-start = (bf16[16,1024]{1,0:T(8,128)(2,1)}, bf16[16,1024]{1,0:T(8,128)(2,1)S(1)}, u32[]{:S(2)}, u32[]{:S(2)}) collective-permute-start(bf16[16,1024]{1,0:T(8,128)(2,1)} %param.9), channel_id=1, source_target_pairs={{0,2},{2,4},{4,6},{6,8},{8,10},{10,12},{12,14},{14,0},{1,3},{3,5},... | collective-permute-start | bytes 98312 | tf_op jit(solution)/shard_map/ppermute | solution.py:21
  9.5 3.0 %collective-permute-start.1 = (bf16[16,1024]{1,0:T(8,128)(2,1)}, bf16[16,1024]{1,0:T(8,128)(2,1)S(1)}, u32[]{:S(2)}, u32[]{:S(2)}) collective-permute-start(bf16[16,1024]{1,0:T(8,128)(2,1)} %param.9), channel_id=1, source_target_pairs={{0,14},{2,0},{4,2},{6,4},{8,6},{10,8},{12,10},{14,12},{1,15},{3,1}... | collective-permute-start | bytes 98312 | tf_op jit(solution)/shard_map/ppermute | solution.py:26
  13.2 0.8 and_convert_fusion
  14.0 0.7 broadcast_in_dim.13
  14.7 1.4 %constant_dynamic-update-slice_fusion.7 = bf16[128,1024]{1,0:T(8,128)(2,1)} fusion(bf16[128,1024]{1,0:T(8,128)(2,1)} %broadcast_in_dim.13, bf16[16,1024]{1,0:T(8,128)(2,1)} %param.9, s32[]{:T(128)S(6)} %select_n.58), kind=kLoop, calls=%fused_computation.37 | loop fusion | bytes 65540 | tf_op jit(solution)/shard_map/dynamic_update_slice | solution.py:17
  16.1 2.1 %copy.14 = bf16[512,512]{0,1:T(8,128)(2,1)} copy(bf16[512,512]{1,0:T(8,128)(2,1)} %param.15) | data formatting | bytes 1048576 | tf_op jit(solution)/shard_map/reshape | solution.py:53
  18.2 2.1 %copy.17 = bf16[128,8,2,512]{3,1,2,0:T(8,128)(2,1)S(1)} copy(bf16[128,8,2,512]{3,2,1,0:T(2,128)(2,1)} %bitcast.29) | data formatting | bytes 4194304
  20.4 0.0 collective-permute-done
  20.4 0.1 collective-permute-start.2
  20.4 0.0 collective-permute-done.1
  20.4 4.7 %collective-permute-start.3 = (bf16[16,1024]{1,0:T(8,128)(2,1)S(1)}, bf16[16,1024]{1,0:T(8,128)(2,1)S(1)}, u32[]{:S(2)}, u32[]{:S(2)}) collective-permute-start(bf16[16,1024]{1,0:T(8,128)(2,1)S(1)} %collective-permute-done.1), channel_id=1, source_target_pairs={{0,14},{2,0},{4,2},{6,4},{8,6},{10,8},{12,10},{14,12},{1,15},{3,1}... | collective-permute-start | bytes 98312 | tf_op jit(solution)/shard_map/ppermute | solution.py:26
  25.1 0.6 constant_dynamic-update-slice_fusion.6
  25.8 0.6 constant_dynamic-update-slice_fusion.5
  26.4 0.7 collective-permute-done.2
  27.0 0.0 collective-permute-start.4
  27.0 0.0 collective-permute-done.3
  27.0 4.7 %collective-permute-start.5 = (bf16[16,1024]{1,0:T(8,128)(2,1)S(1)}, bf16[16,1024]{1,0:T(8,128)(2,1)S(1)}, u32[]{:S(2)}, u32[]{:S(2)}) collective-permute-start(bf16[16,1024]{1,0:T(8,128)(2,1)S(1)} %collective-permute-done.3), channel_id=1, source_target_pairs={{0,14},{2,0},{4,2},{6,4},{8,6},{10,8},{12,10},{14,12},{1,15},{3,1}... | collective-permute-start | bytes 98312 | tf_op jit(solution)/shard_map/ppermute | solution.py:26
  31.8 0.6 constant_dynamic-update-slice_fusion.4
  32.4 0.6 constant_dynamic-update-slice_fusion.3
  33.0 0.7 collective-permute-done.4
  33.6 0.0 collective-permute-start.6
  33.6 0.6 constant_dynamic-update-slice_fusion.2
  34.3 0.0 collective-permute-done.5
  34.3 0.6 constant_dynamic-update-slice_fusion.1
  34.9 5.4 %collective-permute-done.6 = bf16[16,1024]{1,0:T(8,128)(2,1)S(1)} collective-permute-done((bf16[16,1024]{1,0:T(8,128)(2,1)S(1)}, bf16[16,1024]{1,0:T(8,128)(2,1)S(1)}, u32[]{:S(2)}, u32[]{:S(2)}) %collective-permute-start.6) | collective-permute-done | bytes 32800 | tf_op jit(solution)/shard_map/ppermute | solution.py:21
  40.3 0.6 constant_dynamic-update-slice_fusion
  40.9 2.0 %fusion.14 = bf16[16,4,8,128]{3,2,1,0:T(8,128)(2,1)} fusion(bf16[128,1024]{1,0:T(8,128)(2,1)} %constant_dynamic-update-slice_fusion, bf16[1024,1024]{1,0:T(8,128)(2,1)S(1)} %bitcast.27), kind=kOutput, calls=%fused_computation.13 | convolution fusion | flops 134545408 | bytes 1441792 | tf_op jit(solution)/shard_map/dot_general | solution.py:48
  42.8 0.0 copy-start.1
  42.8 0.0 copy-start.2
  42.8 2.6 %fusion.4 = f32[4,128,128]{1,2,0:T(8,128)} fusion(bf16[512,4,128]{0,2,1:T(8,128)(2,1)} %bitcast.30, f32[128,512]{1,0:T(8,128)S(1)} %and_convert_fusion, bf16[16,4,8,128]{3,2,1,0:T(8,128)(2,1)} %fusion.14, bf16[512,512]{1,0:T(8,128)(2,1)} %param.14), kind=kOutput, calls=%fused_computation.6 | convolution fusion | flops 136052736 | bytes 1703936 | tf_op jit(solution)/shard_map/while/body/eval_jaxpr/hce,ehd->chd/dot_general | solution.py:66
  45.5 1.8 %copy.13 = f32[128,512]{1,0:T(8,128)} copy(f32[128,512]{0,1:T(8,128)} %bitcast.31) | data formatting | bytes 524288 | tf_op jit(solution)/shard_map/reshape | solution.py:82
  47.2 0.0 reduce-scatter.2.cloned.1.call-update
  47.3 0.0 all-reduce.3.cloned.1.call-start
  47.3 59.6 %reduce-scatter.2.cloned.1.call-done = f32[16,512]{1,0:T(8,128)} async-done(((f32[128,512]{1,0:T(8,128)}), f32[16,512]{1,0:T(8,128)}) %reduce-scatter.2.cloned.1.call-update) | async-done | bytes 32784 | tf_op jit(solution)/shard_map/reduce_scatter | solution.py:81
  107.0 0.9 fusion.38
  107.8 2.5 %all-reduce = (f32[16]{0:T(128)S(1)}, f32[16]{0:T(128)S(1)}) all-reduce(f32[16]{0:T(128)S(1)} %get-tuple-element.20, f32[16]{0:T(128)S(1)} %get-tuple-element.19), channel_id=1, replica_groups=mesh['groups'=2,'events'=8,'heads'=2] {'heads'}, use_global_device_ids=true, to_apply=%region_4.5 | all-reduce | flops 32 | bytes 256 | tf_op jit(solution)/shard_map/psum | solution.py:89
  110.3 0.0 copy-done
  110.3 0.0 copy-done.1
  110.3 0.0 copy-done.2
  110.3 1.9 %fusion.26 = f32[16,1024]{1,0:T(8,128)} fusion(bf16[512,1024]{1,0:T(8,128)(2,1)S(1)} %copy-done, bf16[16,1024]{1,0:T(8,128)(2,1)S(1)} %copy-done.1, bf16[1024,1024]{1,0:T(8,128)(2,1)S(1)} %bitcast.28, f32[16,512]{1,0:T(8,128)} %reduce-scatter.2.cloned.1.call-done, f32[512]{0:T(512)S(1)} %copy-done.2, f32[16]{0:T(128)S(1)} %get-tuple-element.32, ...), kind=kOutput, calls=%fused_computation.20 | convolution fusion | flops 33644544 | bytes 2231296 | tf_op jit(solution)/shard_map/dot_general | solution.py:94
  112.2 0.0 all-reduce.3.cloned.1.call-update
  112.2 16.9 %all-reduce.3.cloned.1.call-done = f32[16,1024]{1,0:T(8,128)} async-done(((f32[16,1024]{1,0:T(8,128)}), f32[16,1024]{1,0:T(8,128)}) %all-reduce.3.cloned.1.call-update) | async-done | bytes 65552 | tf_op jit(solution)/shard_map/psum | solution.py:95
  129.1 1.5 %add_convert_fusion = bf16[16,1024]{1,0:T(8,128)(2,1)} fusion(f32[16,1024]{1,0:T(8,128)} %all-reduce.3.cloned.1.call-done, bf16[16,1024]{1,0:T(8,128)(2,1)S(1)} %copy-done.1), kind=kLoop, calls=%fused_computation.17 | loop fusion | flops 49152 | bytes 131072 | tf_op jit(solution)/shard_map/convert_element_type | solution.py:96
  (2 shorter events, 0.0 us)
Async XLA Ops:
  6.5 103.8 %copy-start = (bf16[512,1024]{1,0:T(8,128)(2,1)S(1)}, bf16[512,1024]{1,0:T(8,128)(2,1)}, u32[]{:S(2)}) copy-start(bf16[512,1024]{1,0:T(8,128)(2,1)} %param.17) | copy-start | bytes 3145732
  6.5 100.4 %reduce-scatter.2.cloned.1.call-start = ((), (), s32[]{:S(2)}) async-start(), calls=%async_computation.1 | async-start | bytes 294912 | tf_op jit(solution)/shard_map/reduce_scatter | solution.py:81
  6.5 13.8 %collective-permute-start = (bf16[16,1024]{1,0:T(8,128)(2,1)}, bf16[16,1024]{1,0:T(8,128)(2,1)S(1)}, u32[]{:S(2)}, u32[]{:S(2)}) collective-permute-start(bf16[16,1024]{1,0:T(8,128)(2,1)} %param.9), channel_id=1, source_target_pairs={{0,2},{2,4},{4,6},{6,8},{8,10},{10,12},{12,14},{14,0},{1,3},{3,5},... | collective-permute-start | bytes 98312 | tf_op jit(solution)/shard_map/ppermute | solution.py:21
  9.5 10.9 %collective-permute-start.1 = (bf16[16,1024]{1,0:T(8,128)(2,1)}, bf16[16,1024]{1,0:T(8,128)(2,1)S(1)}, u32[]{:S(2)}, u32[]{:S(2)}) collective-permute-start(bf16[16,1024]{1,0:T(8,128)(2,1)} %param.9), channel_id=1, source_target_pairs={{0,14},{2,0},{4,2},{6,4},{8,6},{10,8},{12,10},{14,12},{1,15},{3,1}... | collective-permute-start | bytes 98312 | tf_op jit(solution)/shard_map/ppermute | solution.py:26
  20.4 6.7 %collective-permute-start.2 = (bf16[16,1024]{1,0:T(8,128)(2,1)S(1)}, bf16[16,1024]{1,0:T(8,128)(2,1)S(1)}, u32[]{:S(2)}, u32[]{:S(2)}) collective-permute-start(bf16[16,1024]{1,0:T(8,128)(2,1)S(1)} %collective-permute-done), channel_id=1, source_target_pairs={{0,2},{2,4},{4,6},{6,8},{8,10},{10,12},{12,14},{14,0},{1,3},{3,5},... | collective-permute-start | bytes 98312 | tf_op jit(solution)/shard_map/ppermute | solution.py:21
  20.4 6.6 %collective-permute-start.3 = (bf16[16,1024]{1,0:T(8,128)(2,1)S(1)}, bf16[16,1024]{1,0:T(8,128)(2,1)S(1)}, u32[]{:S(2)}, u32[]{:S(2)}) collective-permute-start(bf16[16,1024]{1,0:T(8,128)(2,1)S(1)} %collective-permute-done.1), channel_id=1, source_target_pairs={{0,14},{2,0},{4,2},{6,4},{8,6},{10,8},{12,10},{14,12},{1,15},{3,1}... | collective-permute-start | bytes 98312 | tf_op jit(solution)/shard_map/ppermute | solution.py:26
  27.0 6.6 %collective-permute-start.4 = (bf16[16,1024]{1,0:T(8,128)(2,1)S(1)}, bf16[16,1024]{1,0:T(8,128)(2,1)S(1)}, u32[]{:S(2)}, u32[]{:S(2)}) collective-permute-start(bf16[16,1024]{1,0:T(8,128)(2,1)S(1)} %collective-permute-done.2), channel_id=1, source_target_pairs={{0,2},{2,4},{4,6},{6,8},{8,10},{10,12},{12,14},{14,0},{1,3},{3,5},... | collective-permute-start | bytes 98312 | tf_op jit(solution)/shard_map/ppermute | solution.py:21
  27.0 7.2 %collective-permute-start.5 = (bf16[16,1024]{1,0:T(8,128)(2,1)S(1)}, bf16[16,1024]{1,0:T(8,128)(2,1)S(1)}, u32[]{:S(2)}, u32[]{:S(2)}) collective-permute-start(bf16[16,1024]{1,0:T(8,128)(2,1)S(1)} %collective-permute-done.3), channel_id=1, source_target_pairs={{0,14},{2,0},{4,2},{6,4},{8,6},{10,8},{12,10},{14,12},{1,15},{3,1}... | collective-permute-start | bytes 98312 | tf_op jit(solution)/shard_map/ppermute | solution.py:26
  33.6 6.6 %collective-permute-start.6 = (bf16[16,1024]{1,0:T(8,128)(2,1)S(1)}, bf16[16,1024]{1,0:T(8,128)(2,1)S(1)}, u32[]{:S(2)}, u32[]{:S(2)}) collective-permute-start(bf16[16,1024]{1,0:T(8,128)(2,1)S(1)} %collective-permute-done.4), channel_id=1, source_target_pairs={{0,2},{2,4},{4,6},{6,8},{8,10},{10,12},{12,14},{14,0},{1,3},{3,5},... | collective-permute-start | bytes 98312 | tf_op jit(solution)/shard_map/ppermute | solution.py:21
  42.8 67.5 %copy-start.1 = (bf16[16,1024]{1,0:T(8,128)(2,1)S(1)}, bf16[16,1024]{1,0:T(8,128)(2,1)}, u32[]{:S(2)}) copy-start(bf16[16,1024]{1,0:T(8,128)(2,1)} %param.9) | copy-start | bytes 98308
  42.8 67.5 %copy-start.2 = (f32[512]{0:T(512)S(1)}, f32[512]{0:T(512)}, u32[]{:S(2)}) copy-start(f32[512]{0:T(512)} %param.16) | copy-start | bytes 6148
  47.3 81.9 %all-reduce.3.cloned.1.call-start = ((), (), s32[]{:S(2)}) async-start(), calls=%async_computation.2 | async-start | bytes 131072 | tf_op jit(solution)/shard_map/psum | solution.py:95
Sparse Core Ops, SparseCore 0:
  47.4 59.5 reduce-scatter.1
  112.3 16.7 all-reduce.2
